TPU v7x, 32 devices: a whole 2x2x4 slice. The times are simulated.
32 devices in a mesh: blk: 4 (over y, x), group: 8 (over z, core).
Axes of the slice: x: 2, y: 2, z: 4, core: 2. Of those that a mesh axis runs over, the one named last changes fastest.
Arguments:
- picture_vector_list: bfloat16 [8, 1024, 768], P('group', 'blk'), may hold values from -0.25 to 0.25
- caption_latent_matrix: bfloat16 [8, 1024, 3072], P('group', 'blk'), may hold values from -6 to 6
- linear_map_matrix: bfloat16 [3072, 768], P('group'), may hold values from -0.109375 to 0.109375
- target_match_index: int32 [8, 1024], P('group', 'blk'), may hold values from 0 to 1023, each once within a row
- sharpness_factor: float32 [1], replicated, may hold values from 24 to 40
- offset_term: float32 [1], replicated, may hold values from -6 to -5
Outputs:
- row_loss: float32 [8, 1024], P('group', 'blk')
- image_grad: bfloat16 [8, 1024, 768], P('group', 'blk')
- projection_grad: float32 [3072, 768], P(('blk', 'group'))
Inputs may be any that keep to these rules, and one draw needn't show every extreme that they name: `target_match_index`: each data group's row of positives is a permutation of 0 to 1023.
All inputs are finite; a program needn't handle non-finite values.
Results may differ from a plain program's by a relative error of at most 0.015.
Values may be sent and summed in bfloat16 or wider, within the bound.
No kernel may reach another device: no remote copies, remote signals or barrier semaphores. Data moves between devices by JAX's collectives and lax.ppermute only.
A program may use at most 64 MiB of HBM per device.

v0:
```python
import jax
import jax.numpy as jnp
from jax import lax
from jax.sharding import PartitionSpec as P

epsilon = 1e-06


def passed_along(value, axis, steps):
    count = lax.axis_size(axis)
    pairs = [(source, (source + steps) % count) for source in range(count)]
    return lax.ppermute(value, axis, pairs)


def body(
    picture_vector_list,
    caption_latent_matrix,
    linear_map_matrix,
    target_match_index,
    sharpness_factor,
    offset_term,
):
    image_rows = picture_vector_list[0]
    hidden_rows = caption_latent_matrix[0]
    label_rows = target_match_index[0]
    row_count = image_rows.shape[0]
    feature_dim = image_rows.shape[1]
    blocks = lax.axis_size("blk")
    my_index = lax.axis_index("blk")
    multiplier_amount = sharpness_factor[0]
    offset_value = offset_term[0]
    columns = hidden_rows
    projected = jnp.dot(
        columns,
        lax.all_gather(linear_map_matrix, "group", axis=0, tiled=True),
        preferred_element_type=jnp.float32,
    )
    text_scale = lax.rsqrt(jnp.sum(projected * projected, axis=1, keepdims=True) + epsilon)
    text_dir = projected * text_scale
    text_unit = text_dir.astype(jnp.bfloat16)
    image_float = image_rows.astype(jnp.float32)
    image_scale = lax.rsqrt(jnp.sum(image_float * image_float, axis=1, keepdims=True) + epsilon)
    image_dir = image_float * image_scale
    image_unit = image_dir.astype(jnp.bfloat16)

    def signed_logits(image_tile_rows, label_block, text_block, column_start):
        columns = column_start + jnp.arange(text_block.shape[0], dtype=jnp.int32)
        pair_sign = jnp.where(label_block[:, None] == columns[None, :], 1.0, -1.0).astype(
            jnp.float32
        )
        pair_scores = lax.dot_general(
            image_tile_rows,
            text_block,
            (((1,), (1,)), ((), ())),
            preferred_element_type=jnp.float32,
        )
        return (multiplier_amount * pair_scores + offset_value, pair_sign)

    def weights_of(logits, pair_sign):
        return (-pair_sign * jax.nn.sigmoid(-pair_sign * logits) * multiplier_amount).astype(
            jnp.bfloat16
        )

    image_unit_grad = jnp.zeros((row_count, feature_dim), jnp.float32)
    loss_local = jnp.zeros((row_count,), jnp.float32)
    text_block = text_unit
    for step_index in range(blocks):
        source = (my_index - step_index) % blocks
        logits, pair_sign = signed_logits(image_unit, label_rows, text_block, source * row_count)
        loss_local = loss_local + -jnp.sum(jax.nn.log_sigmoid(pair_sign * logits), axis=1)
        pair_weight = weights_of(logits, pair_sign)
        image_unit_grad = image_unit_grad + jnp.dot(
            pair_weight, text_block, preferred_element_type=jnp.float32
        )
        if step_index + 1 < blocks:
            text_block = passed_along(text_block, "blk", 1)
    own_start = my_index * row_count
    image_piece = lax.all_gather(image_unit, "blk", axis=0, tiled=True)
    label_piece = lax.all_gather(label_rows, "blk", axis=0, tiled=True)
    logits, pair_sign = signed_logits(image_piece, label_piece, text_unit, own_start)
    pair_weight = weights_of(logits, pair_sign)
    text_unit_grad = lax.dot_general(
        pair_weight, image_piece, (((0,), (0,)), ((), ())), preferred_element_type=jnp.float32
    )
    image_grad = (
        image_scale
        * (
            image_unit_grad
            - image_dir * jnp.sum(image_dir * image_unit_grad, axis=1, keepdims=True)
        )
    ).astype(jnp.bfloat16)
    projection_output_gradient = (
        text_scale
        * (text_unit_grad - text_dir * jnp.sum(text_dir * text_unit_grad, axis=1, keepdims=True))
    ).astype(jnp.bfloat16)
    columns = hidden_rows
    projection_grad = lax.psum_scatter(
        lax.dot_general(
            columns,
            projection_output_gradient,
            (((0,), (0,)), ((), ())),
            preferred_element_type=jnp.float32,
        ),
        ("blk", "group"),
        scatter_dimension=0,
        tiled=True,
    )
    return (loss_local[None], image_grad[None], projection_grad)


def solution(mesh):
    return jax.shard_map(
        body,
        mesh=mesh,
        in_specs=(
            P("group", "blk", None),
            P("group", "blk", None),
            P("group", None),
            P("group", "blk"),
            P(),
            P(),
        ),
        out_specs=(P("group", "blk"), P("group", "blk", None), P(("blk", "group"), None)),
        check_vma=False,
    )
```

profile of v0, /device:TPU:0, one launch (start us, length us, event | category | flops | bytes accessed | tf_op | source)
XLA Modules:
  0.0 257.5 jit_solution(9647050227928517033)
XLA Ops:
  7.2 0.0 all-gather.4.cloned.1.call-start
  7.2 0.7 all-gather.4.cloned.1.call-update
  7.9 0.0 all-gather.6.cloned.1.call-start
  8.0 1.2 fusion.27
  9.1 1.9 fusion.22
  11.0 0.0 reduce-scatter.4.cloned.1.call-start
  12.4 10.1 %all-gather = s32[1,1024]{1,0:T(1,128)} all-gather(s32[1,256]{1,0:T(1,128)S(1)} %copy-done.3), channel_id=2, replica_groups=mesh['blk'=4,'group'=8] {'blk'}, dimensions={1}, use_global_device_ids=true | all-gather | bytes 5120 | tf_op jit(solution)/shard_map/all_gather | solution.py:79
  22.5 0.6 iota_add_fusion
  23.0 41.1 %all-gather.4.cloned.1.call-done = bf16[3072,768]{1,0:T(8,128)(2,1)} async-done(((bf16[384,768]{1,0:T(8,128)(2,1)}), bf16[3072,768]{1,0:T(8,128)(2,1)}) %all-gather.4.cloned.1.call-update) | async-done | bytes 4718608 | tf_op jit(solution)/shard_map/all_gather | solution.py:35
  64.1 3.8 %multiply_reduce_fusion.1 = (f32[256]{0:T(256)S(1)}, f32[256,768]{1,0:T(8,128)S(1)}) fusion(bf16[3072,768]{1,0:T(8,128)(2,1)} %all-gather.4.cloned.1.call-done, bf16[1,256,3072]{2,1,0:T(8,128)(2,1)S(1)} %copy-done), kind=kOutput, calls=%fused_computation.41 | convolution fusion | flops 1208352512 | bytes 7078912 | tf_op jit(solution)/shard_map/dot_general | solution.py:33
  67.9 0.1 multiply_convert_fusion.1
  68.0 28.3 %all-gather.6.cloned.1.call-done = bf16[1024,768]{1,0:T(8,128)(2,1)} async-done(((bf16[256,768]{1,0:T(8,128)(2,1)}), bf16[1024,768]{1,0:T(8,128)(2,1)}) %all-gather.6.cloned.1.call-update) | async-done | bytes 1572880 | tf_op jit(solution)/shard_map/all_gather | solution.py:78
  96.3 3.9 %multiply_reduce_fusion = (f32[256]{0:T(256)S(1)}, f32[256,768]{1,0:T(8,128)S(1)}) fusion(f32[256,768]{1,0:T(8,128)S(1)} %get-tuple-element.14, f32[256]{0:T(256)S(1)} %add_rsqrt_fusion, bf16[1024,768]{1,0:T(8,128)(2,1)} %all-gather.6.cloned.1.call-done, bf16[256,768]{1,0:T(8,128)(2,1)S(1)} %multiply_convert_fusion.1, f32[]{:T(128)} %bitcast.49, ...), kind=kOutput, calls=%fused_computation.40 | convolution fusion | flops 809041664 | bytes 3546120 | tf_op jit(solution)/shard_map/dot_general | solution.py:82
  100.2 5.3 %convolution_bitcast_fusion = f32[3072,768]{0,1:T(8,128)} fusion(bf16[1,256,3072]{2,1,0:T(8,128)(2,1)S(1)} %copy-done, f32[256,768]{1,0:T(8,128)S(1)} %get-tuple-element.19, f32[256,768]{1,0:T(8,128)S(1)} %get-tuple-element.14, f32[256]{0:T(256)S(1)} %get-tuple-element.18, f32[256]{0:T(256)S(1)} %add_rsqrt_fusion), kind=kOutput, calls=%fused_computation | convolution fusion | flops 1208942592 | bytes 12584960 | tf_op jit(solution)/shard_map/dot_general | solution.py:98
  105.5 9.6 %copy.11 = f32[3072,768]{1,0:T(8,128)} copy(f32[3072,768]{0,1:T(8,128)} %convolution_bitcast_fusion) | data formatting | bytes 18874368
  115.2 1.5 collective-permute-start
  116.7 10.3 %collective-permute-done = bf16[256,768]{1,0:T(8,128)(2,1)S(1)} collective-permute-done((bf16[256,768]{1,0:T(8,128)(2,1)S(1)}, bf16[256,768]{1,0:T(8,128)(2,1)S(1)}, u32[]{:S(2)}, u32[]{:S(2)}) %collective-permute-start) | collective-permute-done | bytes 393248 | tf_op jit(solution)/shard_map/ppermute | solution.py:12
  127.0 0.6 collective-permute-start.1
  127.5 0.3 fusion.12
  127.8 10.0 %collective-permute-done.1 = bf16[256,768]{1,0:T(8,128)(2,1)S(1)} collective-permute-done((bf16[256,768]{1,0:T(8,128)(2,1)S(1)}, bf16[256,768]{1,0:T(8,128)(2,1)S(1)}, u32[]{:S(2)}, u32[]{:S(2)}) %collective-permute-start.1) | collective-permute-done | bytes 393248 | tf_op jit(solution)/shard_map/ppermute | solution.py:12
  137.8 0.4 fusion.77
  138.3 0.3 fusion.14
  138.6 9.2 %collective-permute-done.2 = bf16[256,768]{1,0:T(8,128)(2,1)S(1)} collective-permute-done((bf16[256,768]{1,0:T(8,128)(2,1)S(1)}, bf16[256,768]{1,0:T(8,128)(2,1)S(1)}, u32[]{:S(2)}, u32[]{:S(2)}) %collective-permute-start.2) | collective-permute-done | bytes 393248 | tf_op jit(solution)/shard_map/ppermute | solution.py:12
  147.8 0.3 fusion.15
  148.1 0.9 fusion.70
  149.0 0.6 add_add_fusion
  149.6 0.4 convolution_add_fusion.2
  150.0 0.4 convolution_add_fusion.1
  150.5 0.5 copy-done.2
  151.0 0.5 fusion.23
  151.6 1.0 fusion.34
  152.5 98.5 %reduce-scatter.4.cloned.1.call-done = f32[96,768]{1,0:T(8,128)} async-done(((f32[3072,768]{1,0:T(8,128)}), f32[96,768]{1,0:T(8,128)}) %reduce-scatter.4.cloned.1.call-update) | async-done | bytes 294928
  (14 shorter events, 0.1 us)
Async XLA Ops:
  7.2 56.9 %copy-start = (bf16[1,256,3072]{2,1,0:T(8,128)(2,1)S(1)}, bf16[1,256,3072]{2,1,0:T(8,128)(2,1)}, u32[]{:S(2)}) copy-start(bf16[1,256,3072]{2,1,0:T(8,128)(2,1)} %param.7) | copy-start | bytes 4718596
  7.2 5.2 %copy-start.3 = (s32[1,256]{1,0:T(1,128)S(1)}, s32[1,256]{1,0:T(1,128)}, u32[]{:S(2)}) copy-start(s32[1,256]{1,0:T(1,128)} %param.9) | copy-start | bytes 3076
  7.2 56.9 %all-gather.4.cloned.1.call-start = ((), (), s32[]{:S(2)}) async-start(), calls=%async_computation.1 | async-start | bytes 5308416 | tf_op jit(solution)/shard_map/all_gather | solution.py:35
  7.9 88.4 %all-gather.6.cloned.1.call-start = ((), (), s32[]{:S(2)}) async-start(), calls=%async_computation.2 | async-start | bytes 1966080 | tf_op jit(solution)/shard_map/all_gather | solution.py:78
  11.0 240.0 %reduce-scatter.4.cloned.1.call-start = ((), (), s32[]{:S(2)}) async-start(), calls=%async_computation.3 | async-start | bytes 9732096
  115.1 12.4 %copy-start.1 = (bf16[256,768]{1,0:T(8,128)(2,1)S(1)}, bf16[256,768]{1,0:T(8,128)(2,1)}, u32[]{:S(2)}) copy-start(bf16[256,768]{1,0:T(8,128)(2,1)} %fusion.22) | copy-start | bytes 1179652
  115.2 11.8 %collective-permute-start = (bf16[256,768]{1,0:T(8,128)(2,1)S(1)}, bf16[256,768]{1,0:T(8,128)(2,1)S(1)}, u32[]{:S(2)}, u32[]{:S(2)}) collective-permute-start(bf16[256,768]{1,0:T(8,128)(2,1)S(1)} %multiply_convert_fusion.1), channel_id=1, source_target_pairs={{0,8},{8,16},{16,24},{24,0},{1,9},{9,17},{17,25},{25,1},{2,10},{10... | collective-permute-start | bytes 1179656 | tf_op jit(solution)/shard_map/ppermute | solution.py:12
  127.0 10.9 %collective-permute-start.1 = (bf16[256,768]{1,0:T(8,128)(2,1)S(1)}, bf16[256,768]{1,0:T(8,128)(2,1)S(1)}, u32[]{:S(2)}, u32[]{:S(2)}) collective-permute-start(bf16[256,768]{1,0:T(8,128)(2,1)S(1)} %collective-permute-done), channel_id=1, source_target_pairs={{0,8},{8,16},{16,24},{24,0},{1,9},{9,17},{17,25},{25,1},{2,10},{10... | collective-permute-start | bytes 1179656 | tf_op jit(solution)/shard_map/ppermute | solution.py:12
  137.8 10.0 %collective-permute-start.2 = (bf16[256,768]{1,0:T(8,128)(2,1)S(1)}, bf16[256,768]{1,0:T(8,128)(2,1)S(1)}, u32[]{:S(2)}, u32[]{:S(2)}) collective-permute-start(bf16[256,768]{1,0:T(8,128)(2,1)S(1)} %collective-permute-done.1), channel_id=1, source_target_pairs={{0,8},{8,16},{16,24},{24,0},{1,9},{9,17},{17,25},{25,1},{2,10},{10... | collective-permute-start | bytes 1179656 | tf_op jit(solution)/shard_map/ppermute | solution.py:12
  150.0 1.0 copy-start.2
Sparse Core Ops, SparseCore 0:
  9.7 54.3 all-gather.3
  66.5 29.7 all-gather.5
  115.3 135.6 reduce-scatter.3
where the time goes:
time: 258 us
  waiting for transfers between devices  198 us (77%)
  matrix products  16.6 us (6%)
  between operations  15.1 us (6%)
  local copies, waits for them, and re-layouts  10.2 us (4%)
  blocking collectives  10.1 us (4%)
  other arithmetic  5.28 us (2%)
    unnamed x4, waiting for transfers between devices  99.2 us
    all_gather x1, waiting for transfers between devices, body(): lax.all_gather(linear_map_matrix, 'group', axis=0, tiled=True)  41.1 us
    ppermute x3, waiting for transfers between devices, passed_along(): return lax.ppermute(value, axis, pairs)  29.5 us
    all_gather x1, waiting for transfers between devices, body(): image_piece = lax.all_gather(image_unit, 'blk', axis=0, tiled=True)  28.3 us
    unnamed x9, local copies, waits for them, and re-layouts  10.2 us
    all_gather x1, blocking collectives, body(): label_piece = lax.all_gather(label_rows, 'blk', axis=0, tiled=True)  10.1 us
    dot_general x1, matrix products, body(): lax.dot_general(columns, projection_output_gradient, (((0,), (0,)), ((),...  5.27 us
  transfers between devices with their start and end apart: 6, of which 6 were waited for; matrix products, arithmetic and copies ran while one was open for 5% of the time, Pallas kernels for 0%

commit v1 on v0

--- a/solution.py
+++ b/solution.py
@@ -76,7 +76,18 @@
             text_block = passed_along(text_block, "blk", 1)
     own_start = my_index * row_count
     image_piece = lax.all_gather(image_unit, "blk", axis=0, tiled=True)
-    label_piece = lax.all_gather(label_rows, "blk", axis=0, tiled=True)
+    step_out = lax.axis_size("blk")
+    z1 = lax.axis_index("blk")
+    now, y2, a_now = (step_out, z1, label_rows.shape[0])
+    everything, newest = (label_rows, 1)
+    while newest < now:
+        crops = []
+        for rr in range(now):
+            crops.append((rr, (rr - newest) % now))
+        f_next = lax.ppermute(everything, axis_name="blk", perm=crops)
+        everything = jnp.concatenate([everything, f_next], 0)
+        newest = 2 * newest
+    label_piece = jnp.roll(everything, y2 * a_now, 0)
     logits, pair_sign = signed_logits(image_piece, label_piece, text_unit, own_start)
     pair_weight = weights_of(logits, pair_sign)
     text_unit_grad = lax.dot_general(

time: 258 us -> 258 us (level)
  blocking collectives: 10.1 us -> 0 us
  waiting for transfers between devices: 198 us -> 203 us
  starting transfers between devices: 2.2 us -> 6.9 us
    all_gather x1 -> x0, blocking collectives: 10.1 us -> none  [body(): label_piece = lax.all_gather(label_rows, 'blk', axis=0, tiled=True)]
    ppermute x0 -> x2, starting transfers between devices: none -> 4.7 us  [body(): f_next = lax.ppermute(everything, axis_name='blk', perm=crops)]
    ppermute x0 -> x2, waiting for transfers between devices: none -> 2.89 us  [body(): f_next = lax.ppermute(everything, axis_name='blk', perm=crops)]
    unnamed x9 -> x14, local copies, waits for them, and re-layouts: 10.2 us -> 10.2 us
  transfers between devices with their start and end apart: 6 -> 8, of which waited for: 6 -> 7; matrix products, arithmetic and copies ran while one was open for 5% -> 5% of each run, Pallas kernels for 0% -> 0%
where the time goes in v1:
time: 258 us; the launch traced here: 257 us
  waiting for transfers between devices  203 us (79%)
  matrix products  16.6 us (6%)
  between operations  15.2 us (6%)
  local copies, waits for them, and re-layouts  10.9 us (4%)
  starting transfers between devices  6.9 us (3%)
  other arithmetic  5.28 us (2%)
    unnamed x4, waiting for transfers between devices  99.2 us
    all_gather x1, waiting for transfers between devices, body(): lax.all_gather(linear_map_matrix, 'group', axis=0, tiled=True)  42.8 us
    ppermute x3, waiting for transfers between devices, passed_along(): return lax.ppermute(value, axis, pairs)  29.5 us
    all_gather x1, waiting for transfers between devices, body(): image_piece = lax.all_gather(image_unit, 'blk', axis=0, tiled=True)  28.3 us
    unnamed x14, local copies, waits for them, and re-layouts  10.2 us
    dot_general x1, matrix products, body(): lax.dot_general(columns, projection_output_gradient, (((0,), (0,)), ((),...  5.27 us
  transfers between devices with their start and end apart: 8, of which 7 were waited for; matrix products, arithmetic and copies ran while one was open for 5% of the time, Pallas kernels for 0%

profile of v1, /device:TPU:0, one launch (start us, length us, event | category | flops | bytes accessed | tf_op | source)
XLA Modules:
  0.0 257.5 jit_solution(6476372037910542621)
XLA Ops:
  7.2 0.7 all-gather.3.cloned.1.call-update
  8.0 1.2 fusion.27
  9.1 1.9 fusion.22
  11.1 3.9 %collective-permute-start.3 = (s32[256]{0:T(256)S(1)}, s32[256]{0:T(256)S(1)}, u32[]{:S(2)}, u32[]{:S(2)}) collective-permute-start(s32[256]{0:T(256)S(1)} %bitcast.52), channel_id=1, source_target_pairs={{0,24},{8,0},{16,8},{24,16},{1,25},{9,1},{17,9},{25,17},{2,26},{10... | collective-permute-start | bytes 3080 | tf_op jit(solution)/shard_map/ppermute | solution.py:87
  15.0 0.6 iota_add_fusion
  16.9 0.8 collective-permute-start.4
  17.7 2.9 %collective-permute-done.4 = s32[512]{0:T(512)S(1)} collective-permute-done((s32[512]{0:T(512)S(1)}, s32[512]{0:T(512)S(1)}, u32[]{:S(2)}, u32[]{:S(2)}) %collective-permute-start.4) | collective-permute-done | bytes 2080 | tf_op jit(solution)/shard_map/ppermute | solution.py:87
  20.6 0.7 dynamic_slice.4
  21.3 42.8 %all-gather.3.cloned.1.call-done = bf16[3072,768]{1,0:T(8,128)(2,1)} async-done(((bf16[384,768]{1,0:T(8,128)(2,1)}), bf16[3072,768]{1,0:T(8,128)(2,1)}) %all-gather.3.cloned.1.call-update) | async-done | bytes 4718608 | tf_op jit(solution)/shard_map/all_gather | solution.py:35
  64.1 3.8 %multiply_reduce_fusion.1 = (f32[256]{0:T(256)S(1)}, f32[256,768]{1,0:T(8,128)S(1)}) fusion(bf16[3072,768]{1,0:T(8,128)(2,1)} %all-gather.3.cloned.1.call-done, bf16[1,256,3072]{2,1,0:T(8,128)(2,1)S(1)} %copy-done), kind=kOutput, calls=%fused_computation.41 | convolution fusion | flops 1208352512 | bytes 7078912 | tf_op jit(solution)/shard_map/dot_general | solution.py:33
  67.9 0.1 multiply_convert_fusion.1
  68.0 28.3 %all-gather.5.cloned.1.call-done = bf16[1024,768]{1,0:T(8,128)(2,1)} async-done(((bf16[256,768]{1,0:T(8,128)(2,1)}), bf16[1024,768]{1,0:T(8,128)(2,1)}) %all-gather.5.cloned.1.call-update) | async-done | bytes 1572880 | tf_op jit(solution)/shard_map/all_gather | solution.py:78
  96.3 3.9 %multiply_reduce_fusion = (f32[256]{0:T(256)S(1)}, f32[256,768]{1,0:T(8,128)S(1)}) fusion(f32[256,768]{1,0:T(8,128)S(1)} %get-tuple-element.14, f32[256]{0:T(256)S(1)} %add_rsqrt_fusion, bf16[1024,768]{1,0:T(8,128)(2,1)} %all-gather.5.cloned.1.call-done, bf16[256,768]{1,0:T(8,128)(2,1)S(1)} %multiply_convert_fusion.1, f32[]{:T(128)} %bitcast.48, ...), kind=kOutput, calls=%fused_computation.40 | convolution fusion | flops 809041664 | bytes 3546120 | tf_op jit(solution)/shard_map/dot_general | solution.py:93
  100.2 5.3 %convolution_bitcast_fusion = f32[3072,768]{0,1:T(8,128)} fusion(bf16[1,256,3072]{2,1,0:T(8,128)(2,1)S(1)} %copy-done, f32[256,768]{1,0:T(8,128)S(1)} %get-tuple-element.19, f32[256,768]{1,0:T(8,128)S(1)} %get-tuple-element.14, f32[256]{0:T(256)S(1)} %get-tuple-element.18, f32[256]{0:T(256)S(1)} %add_rsqrt_fusion), kind=kOutput, calls=%fused_computation | convolution fusion | flops 1208942592 | bytes 12584960 | tf_op jit(solution)/shard_map/dot_general | solution.py:109
  105.5 9.6 %copy.11 = f32[3072,768]{1,0:T(8,128)} copy(f32[3072,768]{0,1:T(8,128)} %convolution_bitcast_fusion) | data formatting | bytes 18874368
  115.2 1.5 collective-permute-start
  116.7 10.3 %collective-permute-done = bf16[256,768]{1,0:T(8,128)(2,1)S(1)} collective-permute-done((bf16[256,768]{1,0:T(8,128)(2,1)S(1)}, bf16[256,768]{1,0:T(8,128)(2,1)S(1)}, u32[]{:S(2)}, u32[]{:S(2)}) %collective-permute-start) | collective-permute-done | bytes 393248 | tf_op jit(solution)/shard_map/ppermute | solution.py:12
  127.0 0.6 collective-permute-start.1
  127.5 0.3 fusion.12
  127.8 10.0 %collective-permute-done.1 = bf16[256,768]{1,0:T(8,128)(2,1)S(1)} collective-permute-done((bf16[256,768]{1,0:T(8,128)(2,1)S(1)}, bf16[256,768]{1,0:T(8,128)(2,1)S(1)}, u32[]{:S(2)}, u32[]{:S(2)}) %collective-permute-start.1) | collective-permute-done | bytes 393248 | tf_op jit(solution)/shard_map/ppermute | solution.py:12
  137.8 0.4 fusion.77
  138.3 0.3 fusion.14
  138.6 9.2 %collective-permute-done.2 = bf16[256,768]{1,0:T(8,128)(2,1)S(1)} collective-permute-done((bf16[256,768]{1,0:T(8,128)(2,1)S(1)}, bf16[256,768]{1,0:T(8,128)(2,1)S(1)}, u32[]{:S(2)}, u32[]{:S(2)}) %collective-permute-start.2) | collective-permute-done | bytes 393248 | tf_op jit(solution)/shard_map/ppermute | solution.py:12
  147.8 0.3 fusion.15
  148.1 0.9 fusion.70
  149.0 0.6 add_add_fusion
  149.6 0.4 convolution_add_fusion.2
  150.0 0.4 convolution_add_fusion.1
  150.5 0.5 copy-done.2
  151.0 0.5 fusion.23
  151.6 1.0 fusion.34
  152.5 98.4 %reduce-scatter.4.cloned.1.call-done = f32[96,768]{1,0:T(8,128)} async-done(((f32[3072,768]{1,0:T(8,128)}), f32[96,768]{1,0:T(8,128)}) %reduce-scatter.4.cloned.1.call-update) | async-done | bytes 294928
  (26 shorter events, 0.2 us)
Async XLA Ops:
  7.2 56.9 %copy-start = (bf16[1,256,3072]{2,1,0:T(8,128)(2,1)S(1)}, bf16[1,256,3072]{2,1,0:T(8,128)(2,1)}, u32[]{:S(2)}) copy-start(bf16[1,256,3072]{2,1,0:T(8,128)(2,1)} %param.7) | copy-start | bytes 4718596
  7.2 3.9 %copy-start.3 = (s32[1,256]{1,0:T(1,128)S(1)}, s32[1,256]{1,0:T(1,128)}, u32[]{:S(2)}) copy-start(s32[1,256]{1,0:T(1,128)} %param.9) | copy-start | bytes 3076
  7.2 56.9 %all-gather.3.cloned.1.call-start = ((), (), s32[]{:S(2)}) async-start(), calls=%async_computation.1 | async-start | bytes 5308416 | tf_op jit(solution)/shard_map/all_gather | solution.py:35
  7.9 88.4 %all-gather.5.cloned.1.call-start = ((), (), s32[]{:S(2)}) async-start(), calls=%async_computation.2 | async-start | bytes 1966080 | tf_op jit(solution)/shard_map/all_gather | solution.py:78
  11.0 239.9 %reduce-scatter.4.cloned.1.call-start = ((), (), s32[]{:S(2)}) async-start(), calls=%async_computation.3 | async-start | bytes 9732096
  11.1 5.8 %collective-permute-start.3 = (s32[256]{0:T(256)S(1)}, s32[256]{0:T(256)S(1)}, u32[]{:S(2)}, u32[]{:S(2)}) collective-permute-start(s32[256]{0:T(256)S(1)} %bitcast.52), channel_id=1, source_target_pairs={{0,24},{8,0},{16,8},{24,16},{1,25},{9,1},{17,9},{25,17},{2,26},{10... | collective-permute-start | bytes 3080 | tf_op jit(solution)/shard_map/ppermute | solution.py:87
  16.9 3.7 %collective-permute-start.4 = (s32[512]{0:T(512)S(1)}, s32[512]{0:T(512)S(1)}, u32[]{:S(2)}, u32[]{:S(2)}) collective-permute-start(s32[512]{0:T(512)S(1)} %pad_add_fusion), channel_id=1, source_target_pairs={{0,16},{8,24},{16,0},{24,8},{1,17},{9,25},{17,1},{25,9},{2,18},{10... | collective-permute-start | bytes 6152 | tf_op jit(solution)/shard_map/ppermute | solution.py:87
  115.1 12.4 %copy-start.1 = (bf16[256,768]{1,0:T(8,128)(2,1)S(1)}, bf16[256,768]{1,0:T(8,128)(2,1)}, u32[]{:S(2)}) copy-start(bf16[256,768]{1,0:T(8,128)(2,1)} %fusion.22) | copy-start | bytes 1179652
  115.2 11.8 %collective-permute-start = (bf16[256,768]{1,0:T(8,128)(2,1)S(1)}, bf16[256,768]{1,0:T(8,128)(2,1)S(1)}, u32[]{:S(2)}, u32[]{:S(2)}) collective-permute-start(bf16[256,768]{1,0:T(8,128)(2,1)S(1)} %multiply_convert_fusion.1), channel_id=1, source_target_pairs={{0,8},{8,16},{16,24},{24,0},{1,9},{9,17},{17,25},{25,1},{2,10},{10... | collective-permute-start | bytes 1179656 | tf_op jit(solution)/shard_map/ppermute | solution.py:12
  127.0 10.9 %collective-permute-start.1 = (bf16[256,768]{1,0:T(8,128)(2,1)S(1)}, bf16[256,768]{1,0:T(8,128)(2,1)S(1)}, u32[]{:S(2)}, u32[]{:S(2)}) collective-permute-start(bf16[256,768]{1,0:T(8,128)(2,1)S(1)} %collective-permute-done), channel_id=1, source_target_pairs={{0,8},{8,16},{16,24},{24,0},{1,9},{9,17},{17,25},{25,1},{2,10},{10... | collective-permute-start | bytes 1179656 | tf_op jit(solution)/shard_map/ppermute | solution.py:12
  137.8 10.0 %collective-permute-start.2 = (bf16[256,768]{1,0:T(8,128)(2,1)S(1)}, bf16[256,768]{1,0:T(8,128)(2,1)S(1)}, u32[]{:S(2)}, u32[]{:S(2)}) collective-permute-start(bf16[256,768]{1,0:T(8,128)(2,1)S(1)} %collective-permute-done.1), channel_id=1, source_target_pairs={{0,8},{8,16},{16,24},{24,0},{1,9},{9,17},{17,25},{25,1},{2,10},{10... | collective-permute-start | bytes 1179656 | tf_op jit(solution)/shard_map/ppermute | solution.py:12
  150.0 1.0 copy-start.2
Sparse Core Ops, SparseCore 0:
  9.7 54.3 all-gather.2
  66.5 29.7 all-gather.4
  115.3 135.6 reduce-scatter.3
